TPU v7x, 32 devices: a whole 2x2x4 slice. The times are simulated.
32 devices in a mesh: grp: 2 (over y), seq: 4 (over z), mdl: 4 (over x, core).
Axes of the slice: x: 2, y: 2, z: 4, core: 2. Of those that a mesh axis runs over, the one named last changes fastest.
Arguments:
- query_proj: bfloat16 [2048, 4096], P(('grp', 'seq'), 'mdl'), parts along dimension 0, may hold values from -12 to 12, as said below
- key_proj: bfloat16 [2048, 4096], P(('grp', 'seq'), 'mdl'), parts along dimension 0, may hold values from -6 to 6
- value_proj: bfloat16 [2048, 4096], P(('grp', 'seq'), 'mdl'), parts along dimension 0, may hold values from -12 to 12, as said below
- gate_proj: bfloat16 [2048, 4096], P(('grp', 'seq'), 'mdl'), parts along dimension 0, may hold values from -6 to 6
- log_decay: float32 [32, 2048], P('mdl', ('grp', 'seq')), parts along dimension 1, may hold values from -2 to 0, as said below
- act_exponent: int32 [3, 4096], P(None, 'mdl'), may hold values from -5 to -2
- norm_gain: float32 [4096], P('mdl'), may hold values from 0.1 to 1.9
- out_weight: bfloat16 [4096, 6144], P('seq', 'mdl'), may hold values from -0.09375 to 0.09375
- weight_exponent: int32 [6144], P('mdl'), may hold values from -12 to -9
Outputs:
- layer_out: bfloat16 [2048, 6144], P(('grp', 'seq'), 'mdl'), parts along dimension 0
There are 2 independent parts, one for each index of `grp`. A program takes and returns all parts, laid end to end along the dimension named above; an argument that names none is the same for every part. Nothing has to cross between parts.
Inputs may be any that keep to these rules, and one draw needn't show every extreme that they name: Rows of query_proj differ in scale. Columns of value_proj differ in scale. `log_decay`: negative everywhere.
All inputs are finite; a program needn't handle non-finite values.
Results may differ from a plain program's by a relative error of at most 0.0062.
Values may be sent and summed in bfloat16 or wider, within the bound.
No kernel may reach another device: no remote copies, remote signals or barrier semaphores. Data moves between devices by JAX's collectives and lax.ppermute only.
A program may use at most 64 MiB of HBM per device.

v0:
```python
import jax
import jax.numpy as jnp
from jax import lax
from jax.sharding import PartitionSpec as P

HDIM = 128
BLK = 256


def power_two(exponent):
    result = jnp.zeros(exponent.shape, jnp.float32)
    for exponent_value in range(-16, 0):
        result = result + jnp.where(exponent == exponent_value, 2.0**exponent_value, 0.0)
    return result


def fake_quant(matrix, exponent):
    scale = power_two(exponent)
    levels = jnp.clip(jnp.floor(matrix.astype(jnp.float32) / scale + 0.5), -127.0, 127.0)
    return (levels * scale).astype(jnp.bfloat16)


def per_device(
    query_proj,
    key_proj,
    value_proj,
    gate_proj,
    log_decay,
    act_exponent,
    norm_gain,
    out_weight,
    weight_exponent,
):
    weights = fake_quant(out_weight, weight_exponent[None, :])
    panels = lax.all_gather(weights, "seq", axis=0, tiled=True)
    tok_rows = query_proj.shape[0]
    heads_here = log_decay.shape[0]
    nblocks = tok_rows // BLK
    queries = fake_quant(query_proj, act_exponent[0][None, :])
    keys_quant = fake_quant(key_proj, act_exponent[1][None, :])
    values = fake_quant(value_proj, act_exponent[2][None, :]).reshape(
        nblocks, BLK, heads_here, HDIM
    )
    query_feat = (
        jax.nn.silu(queries.astype(jnp.float32))
        .astype(jnp.bfloat16)
        .reshape(nblocks, BLK, heads_here, HDIM)
    )
    key_feat = (
        jax.nn.silu(keys_quant.astype(jnp.float32))
        .astype(jnp.bfloat16)
        .reshape(nblocks, BLK, heads_here, HDIM)
    )
    decay_cum = jnp.cumsum(log_decay.reshape(heads_here, nblocks, BLK), axis=2)
    block_total = decay_cum[:, :, -1]
    scores = jnp.einsum("bihd,bjhd->hbij", query_feat, key_feat, preferred_element_type=jnp.float32)
    decay_gap = decay_cum[:, :, :, None] - decay_cum[:, :, None, :]
    causal_mask = jnp.arange(BLK)[:, None] >= jnp.arange(BLK)[None, :]
    decay_mask = jnp.where(causal_mask, jnp.exp(jnp.minimum(decay_gap, 0.0)), 0.0)
    block_probs = (scores * decay_mask).astype(jnp.bfloat16)
    within_block = jnp.einsum(
        "hbij,bjhd->bihd", block_probs, values, preferred_element_type=jnp.float32
    )
    tail_decay = jnp.transpose(jnp.exp(block_total[:, :, None] - decay_cum), (1, 2, 0))
    weighted = (key_feat.astype(jnp.float32) * tail_decay[..., None]).astype(jnp.bfloat16)
    block_states = jnp.einsum(
        "bjhd,bjhe->bhde", weighted, values, preferred_element_type=jnp.float32
    )
    block_gain = jnp.exp(block_total).T

    def advance(carried, inputs):
        gain_here, state_here = inputs
        return (gain_here[:, None, None] * carried + state_here, carried)

    local_end, entry_local = lax.scan(
        advance, jnp.zeros((heads_here, HDIM, HDIM), jnp.float32), (block_gain, block_states)
    )
    device_log = jnp.sum(block_total, axis=1)
    gathered_logs, gathered_states = (
        lax.all_gather(device_log[None], "seq", axis=0, tiled=True),
        lax.all_gather(local_end[None], "seq", axis=0, tiled=True),
    )
    position = lax.axis_index("seq")
    end_offsets = jnp.cumsum(gathered_logs, axis=0)
    start_offsets = end_offsets - gathered_logs
    own_start = lax.dynamic_index_in_dim(start_offsets, position, 0, keepdims=False)
    earlier = jnp.arange(gathered_logs.shape[0])[:, None] < position
    state_weight = jnp.where(
        earlier, jnp.exp(jnp.minimum(own_start[None, :] - end_offsets, 0.0)), 0.0
    )
    incoming = jnp.einsum(
        "nh,nhde->hde", state_weight, gathered_states, precision=lax.Precision.HIGHEST
    )
    before = jnp.cumsum(block_total, axis=1) - block_total
    entry_state = entry_local + jnp.exp(before).T[:, :, None, None] * incoming[None]
    from_state = jnp.einsum(
        "bihd,bhde->bihe",
        query_feat.astype(jnp.float32),
        entry_state,
        precision=lax.Precision.HIGHEST,
    )
    position_decay = jnp.transpose(jnp.exp(decay_cum), (1, 2, 0))[..., None]
    attended = within_block + position_decay * from_state
    mean_square = jnp.mean(attended * attended, axis=-1, keepdims=True)
    normed = (attended * lax.rsqrt(mean_square + 1e-05)).reshape(tok_rows, heads_here * HDIM)
    attn = (normed * norm_gain[None, :] * jax.nn.sigmoid(gate_proj.astype(jnp.float32))).astype(
        jnp.bfloat16
    )
    result = jnp.dot(
        lax.all_gather(attn, "mdl", axis=1, tiled=True), panels, preferred_element_type=jnp.float32
    )
    return result.astype(jnp.bfloat16)


def solution(mesh):
    in_specs = (
        P(("grp", "seq"), "mdl"),
        P(("grp", "seq"), "mdl"),
        P(("grp", "seq"), "mdl"),
        P(("grp", "seq"), "mdl"),
        P("mdl", ("grp", "seq")),
        P(None, "mdl"),
        P("mdl"),
        P("seq", "mdl"),
        P("mdl"),
    )
    out_specs = P(("grp", "seq"), "mdl")
    return jax.shard_map(
        per_device, mesh=mesh, in_specs=in_specs, out_specs=out_specs, check_vma=False
    )
```

profile of v0, /device:TPU:0, one launch (start us, length us, event | category | flops | bytes accessed | tf_op | source)
XLA Modules:
  0.0 324.8 jit_solution(14562951297802620466)
XLA Ops:
  6.5 0.0 all-gather.10.cloned.1.call-start
  6.5 1.2 reduce-window.6
  7.8 0.2 slice_reduce_fusion
  8.0 0.1 exponential_bitcast_fusion.1
  8.1 0.2 multiply_reduce_fusion.2
  8.3 0.1 exponential_bitcast_fusion
  8.3 1.0 fusion.45
  9.3 1.4 fusion.11
  10.8 0.2 copy.49
  11.0 0.0 copy-start.5
  11.0 0.0 copy-start.3
  11.0 0.0 copy-start.4
  11.0 2.4 convolution_add_fusion
  13.4 0.0 all-gather.10.cloned.1.call-update
  13.4 0.0 all-gather.6.cloned.1.call-start
  13.5 0.0 copy-done.5
  13.5 0.6 dynamic-slice.1
  14.7 0.2 dynamic-update-slice
  15.0 13.6 %all-reduce = f32[32]{0:T(128)S(1)} all-reduce(f32[32]{0:T(128)S(1)} %dynamic-update-slice), channel_id=2, replica_groups=mesh['grp'=2,'seq'=4,'mdl'=4] {'seq'}, use_global_device_ids=true, to_apply=%add | all-reduce | flops 32 | bytes 256
  28.6 0.1 reshape.291
  28.8 0.1 select_bitcast_fusion
  28.9 0.1 bitcast_add_fusion.1
  28.9 0.0 copy-done.3
  28.9 0.0 copy-done.4
  28.9 1.4 fusion.1
  30.3 32.0 %all-gather.10.cloned.1.call-done = f32[32,128,128]{2,1,0:T(8,128)} async-done(((f32[8,128,128]{2,1,0:T(8,128)}), f32[32,128,128]{2,1,0:T(8,128)}) %all-gather.10.cloned.1.call-update) | async-done | bytes 2097168 | tf_op jit(solution)/shard_map/all_gather | solution.py:81
  62.3 1.9 multiply_reduce_fusion
  64.2 0.2 copy.47
  64.4 1.0 multiply_reduce_fusion.1
  65.4 0.0 copy-start
  65.4 0.0 copy-start.2
  65.5 0.0 copy-start.1
  65.5 0.1 broadcast_multiply_fusion
  65.6 0.3 copy.40
  65.9 0.6 copy-done
  66.5 0.0 copy-done.2
  66.5 1.1 multiply_convert_fusion.2
  67.6 0.0 all-gather.6.cloned.1.call-update
  67.6 0.0 all-gather.8.cloned.1.call-start
  67.6 0.0 copy-done.1
  67.7 4.1 %multiply_convert_fusion = bf16[1024,1536]{1,0:T(8,128)(2,1)} fusion(bf16[1024,1536]{1,0:T(8,128)(2,1)} %param.16, f32[1536]{0:T(1024)S(1)} %select_add_fusion), kind=kLoop, calls=%fused_computation | loop fusion | flops 11010048 | bytes 6297600 | tf_op jit(solution)/shard_map/convert_element_type | solution.py:20
  71.8 0.0 all-gather.8.cloned.1.call-update
  71.8 17.2 %all-gather.6.cloned.1.call-done = bf16[256,4096]{1,0:T(8,128)(2,1)} async-done(((bf16[256,1024]{1,0:T(8,128)(2,1)}), bf16[256,4096]{1,0:T(8,128)(2,1)}) %all-gather.6.cloned.1.call-update) | async-done | bytes 2097168 | tf_op jit(solution)/shard_map/all_gather | solution.py:110
  89.0 219.8 %all-gather.8.cloned.1.call-done = bf16[4096,1536]{1,0:T(8,128)(2,1)} async-done(((bf16[1024,1536]{1,0:T(8,128)(2,1)}), bf16[4096,1536]{1,0:T(8,128)(2,1)}) %all-gather.8.cloned.1.call-update) | async-done | bytes 12582928 | tf_op jit(solution)/shard_map/all_gather | solution.py:35
  308.8 9.5 %convolution_convert_fusion = bf16[256,1536]{1,0:T(8,128)(2,1)} fusion(bf16[256,4096]{1,0:T(8,128)(2,1)} %all-gather.6.cloned.1.call-done, bf16[4096,1536]{1,0:T(8,128)(2,1)} %all-gather.8.cloned.1.call-done), kind=kOutput, calls=%fused_computation.1 | convolution fusion | flops 3221618688 | bytes 15466496 | tf_op jit(solution)/shard_map/dot_general | solution.py:109
  (11 shorter events, 0.2 us)
Async XLA Ops:
  6.5 55.8 %all-gather.10.cloned.1.call-start = ((), (), s32[]{:S(2)}) async-start(), calls=%async_computation.2 | async-start | bytes 2621440 | tf_op jit(solution)/shard_map/all_gather | solution.py:81
  11.0 2.5 copy-start.5
  11.0 17.9 %copy-start.3 = (bf16[256,1024]{1,0:T(8,128)(2,1)S(1)}, bf16[256,1024]{1,0:T(8,128)(2,1)}, u32[]{:S(2)}) copy-start(bf16[256,1024]{1,0:T(8,128)(2,1)} %param.11) | copy-start | bytes 1572868
  11.0 17.9 %copy-start.4 = (bf16[256,1024]{1,0:T(8,128)(2,1)S(1)}, bf16[256,1024]{1,0:T(8,128)(2,1)}, u32[]{:S(2)}) copy-start(bf16[256,1024]{1,0:T(8,128)(2,1)} %param.9) | copy-start | bytes 1572868
  13.4 75.6 %all-gather.6.cloned.1.call-start = ((), (), s32[]{:S(2)}) async-start(), calls=%async_computation | async-start | bytes 2621440 | tf_op jit(solution)/shard_map/all_gather | solution.py:110
  65.4 1.0 copy-start
  65.4 1.0 copy-start.2
  65.5 2.2 copy-start.1
  67.6 241.2 %all-gather.8.cloned.1.call-start = ((), (), s32[]{:S(2)}) async-start(), calls=%async_computation.1 | async-start | bytes 15728640 | tf_op jit(solution)/shard_map/all_gather | solution.py:35
Sparse Core Ops, SparseCore 0:
  13.6 48.6 all-gather.9
  67.7 21.2 all-gather.5
  90.6 218.2 all-gather.7
where the time goes:
time: 325 us
  waiting for transfers between devices  269 us (83%)
  matrix products  14.3 us (4%)
  between operations  13.9 us (4%)
  blocking collectives  13.6 us (4%)
  other arithmetic  11.5 us (4%)
    all_gather x1, waiting for transfers between devices, per_device(): panels = lax.all_gather(weights, 'seq', axis=0, tiled=True)  220 us
    all_gather x1, waiting for transfers between devices, per_device(): lax.all_gather(local_end[None], 'seq', axis=0, tiled=True)  32 us
    all_gather x1, waiting for transfers between devices, per_device(): lax.all_gather(attn, 'mdl', axis=1, tiled=True)  17.2 us
    unnamed x1, blocking collectives  13.6 us
    dot_general x1, matrix products, per_device(): jnp.dot(lax.all_gather(attn, 'mdl', axis=1, tiled=True), panels, preferre...  9.5 us
  transfers between devices with their start and end apart: 3, of which 3 were waited for; matrix products, arithmetic and copies ran while one was open for 2% of the time, Pallas kernels for 0%

commit v1 on v0

--- a/solution.py
+++ b/solution.py
@@ -5,6 +5,19 @@
 
 HDIM = 128
 BLK = 256
+
+
+def ring_gather(array, axis, dim):
+    ways = lax.axis_size(axis)
+    up = [(d, (d + 1) % ways) for d in range(ways)]
+    down = [(d, (d - 1) % ways) for d in range(ways)]
+    earlier, later = ([array], [array])
+    for _ in range(ways // 2):
+        earlier.append(lax.ppermute(earlier[-1], axis, up))
+    for _ in range((ways - 1) // 2):
+        later.append(lax.ppermute(later[-1], axis, down))
+    line = jnp.concatenate([*earlier[::-1], *later[1:]], axis=dim)
+    return jnp.roll(line, (lax.axis_index(axis) - ways // 2) * array.shape[dim], axis=dim)
 
 
 def power_two(exponent):
@@ -106,9 +119,7 @@
     attn = (normed * norm_gain[None, :] * jax.nn.sigmoid(gate_proj.astype(jnp.float32))).astype(
         jnp.bfloat16
     )
-    result = jnp.dot(
-        lax.all_gather(attn, "mdl", axis=1, tiled=True), panels, preferred_element_type=jnp.float32
-    )
+    result = jnp.dot(ring_gather(attn, "mdl", 1), panels, preferred_element_type=jnp.float32)
     return result.astype(jnp.bfloat16)
 
 

time: 325 us -> 300 us (0.923)
  waiting for transfers between devices: 269 us -> 233 us
  local copies, waits for them, and re-layouts: 2.43 us -> 11.4 us
    all_gather x1, waiting for transfers between devices: 220 us -> 186 us  [per_device(): panels = lax.all_gather(weights, 'seq', axis=0, tiled=True)]
    ppermute x0 -> x3, waiting for transfers between devices: none -> 19.2 us  [the longest x2 19.2 us: ring_gather(): earlier.append(lax.ppermute(earlier[-1], axis, up))]
    all_gather x1 -> x0, waiting for transfers between devices: 17.2 us -> none  [per_device(): lax.all_gather(attn, 'mdl', axis=1, tiled=True)]
    unnamed x15 -> x22, local copies, waits for them, and re-layouts: 1.45 us -> 7.64 us
    all_gather x1, waiting for transfers between devices: 32 us -> 27.7 us  [per_device(): lax.all_gather(local_end[None], 'seq', axis=0, tiled=True)]
  transfers between devices with their start and end apart: 3 -> 5, of which waited for: 3 -> 4; matrix products, arithmetic and copies ran while one was open for 2% -> 6% of each run, Pallas kernels for 0% -> 0%
where the time goes in v1:
time: 300 us
  waiting for transfers between devices  233 us (78%)
  matrix products  15.8 us (5%)
  between operations  14.2 us (5%)
  blocking collectives  13.6 us (5%)
  local copies, waits for them, and re-layouts  11.4 us (4%)
  other arithmetic  10.2 us (3%)
    all_gather x1, waiting for transfers between devices, per_device(): panels = lax.all_gather(weights, 'seq', axis=0, tiled=True)  186 us
    all_gather x1, waiting for transfers between devices, per_device(): lax.all_gather(local_end[None], 'seq', axis=0, tiled=True)  27.7 us
    ppermute x2, waiting for transfers between devices, ring_gather(): earlier.append(lax.ppermute(earlier[-1], axis, up))  19.2 us
    unnamed x1, blocking collectives  13.6 us
    dot_general x1, matrix products, per_device(): jnp.dot(ring_gather(attn, 'mdl', 1), panels, preferred_element_type=jnp.f...  9.5 us
    unnamed x22, local copies, waits for them, and re-layouts  7.64 us
  transfers between devices with their start and end apart: 5, of which 4 were waited for; matrix products, arithmetic and copies ran while one was open for 6% of the time, Pallas kernels for 0%

profile of v1, /device:TPU:0, one launch (start us, length us, event | category | flops | bytes accessed | tf_op | source)
XLA Modules:
  0.0 300.1 jit_solution(17461921921547974168)
XLA Ops:
  6.5 1.2 reduce-window.6
  7.8 0.2 slice_reduce_fusion
  8.0 0.1 exponential_bitcast_fusion.1
  8.1 0.2 multiply_reduce_fusion.2
  8.3 0.1 exponential_bitcast_fusion
  8.3 1.0 fusion.46
  9.3 0.0 copy-start.2
  9.3 0.0 copy-start
  9.4 2.4 fusion.12
  11.7 2.1 copy.49
  13.8 2.5 convolution_add_fusion
  16.3 0.0 all-gather.7.cloned.1.call-update
  16.3 0.0 all-gather.5.cloned.1.call-start
  16.4 0.0 copy-start.5
  16.4 2.7 multiply_convert_fusion
  19.1 0.0 all-gather.5.cloned.1.call-update
  19.2 0.6 dynamic-slice.1
  20.5 0.2 dynamic-update-slice
  20.7 13.6 %all-reduce = f32[32]{0:T(128)S(1)} all-reduce(f32[32]{0:T(128)S(1)} %dynamic-update-slice), channel_id=2, replica_groups=mesh['grp'=2,'seq'=4,'mdl'=4] {'seq'}, use_global_device_ids=true, to_apply=%add | all-reduce | flops 32 | bytes 256
  34.3 0.1 reshape.291
  34.5 0.1 select_bitcast_fusion
  34.6 0.1 bitcast_add_fusion.1
  34.7 2.8 fusion.2
  37.5 27.7 %all-gather.7.cloned.1.call-done = f32[32,128,128]{2,1,0:T(8,128)} async-done(((f32[8,128,128]{2,1,0:T(8,128)}), f32[32,128,128]{2,1,0:T(8,128)}) %all-gather.7.cloned.1.call-update) | async-done | bytes 2097168 | tf_op jit(solution)/shard_map/all_gather | solution.py:94
  65.2 1.9 multiply_reduce_fusion
  67.0 0.2 copy.47
  67.3 1.1 multiply_reduce_fusion.1
  68.3 0.0 copy-start.1
  68.3 0.0 copy-start.3
  68.4 0.1 broadcast_multiply_fusion
  68.4 0.3 copy.40
  68.8 0.6 copy-done.1
  69.4 0.3 multiply_convert_fusion.2
  69.7 0.1 collective-permute-start
  69.7 8.6 %collective-permute-done = bf16[256,1024]{1,0:T(8,128)(2,1)S(1)} collective-permute-done((bf16[256,1024]{1,0:T(8,128)(2,1)S(1)}, bf16[256,1024]{1,0:T(8,128)(2,1)S(1)}, u32[]{:S(2)}, u32[]{:S(2)}) %collective-permute-start) | collective-permute-done | bytes 524320 | tf_op jit(solution)/shard_map/ppermute | solution.py:16
  78.3 1.7 collective-permute-start.2
  80.1 10.6 %collective-permute-done.1 = bf16[256,1024]{1,0:T(8,128)(2,1)S(1)} collective-permute-done((bf16[256,1024]{1,0:T(8,128)(2,1)S(1)}, bf16[256,1024]{1,0:T(8,128)(2,1)S(1)}, u32[]{:S(2)}, u32[]{:S(2)}) %collective-permute-start.1) | collective-permute-done | bytes 524320 | tf_op jit(solution)/shard_map/ppermute | solution.py:16
  90.7 0.9 constant_dynamic-update-slice_fusion.7
  91.6 0.9 constant_dynamic-update-slice_fusion.6
  92.5 0.9 constant_dynamic-update-slice_fusion.5
  93.4 0.0 collective-permute-done.2
  93.4 0.8 constant_dynamic-update-slice_fusion.4
  94.3 0.9 constant_dynamic-update-slice_fusion.3
  95.1 0.9 constant_dynamic-update-slice_fusion.2
  96.0 0.9 constant_dynamic-update-slice_fusion.1
  96.9 0.9 constant_dynamic-update-slice_fusion
  97.8 186.0 %all-gather.5.cloned.1.call-done = bf16[4096,1536]{1,0:T(8,128)(2,1)} async-done(((bf16[1024,1536]{1,0:T(8,128)(2,1)}), bf16[4096,1536]{1,0:T(8,128)(2,1)}) %all-gather.5.cloned.1.call-update) | async-done | bytes 12582928 | tf_op jit(solution)/shard_map/all_gather | solution.py:48
  283.7 9.5 %convolution_convert_fusion = bf16[256,1536]{1,0:T(8,128)(2,1)} fusion(bf16[4096,1536]{1,0:T(8,128)(2,1)} %all-gather.5.cloned.1.call-done, bf16[256,8192]{1,0:T(8,128)(2,1)} %constant_dynamic-update-slice_fusion, s32[]{:T(128)S(6)} %select_n.288), kind=kOutput, calls=%fused_computation.1 | convolution fusion | flops 3221618688 | bytes 15466500 | tf_op jit(solution)/shard_map/dot_general | solution.py:122
  (19 shorter events, 0.2 us)
Async XLA Ops:
  6.5 58.6 %all-gather.7.cloned.1.call-start = ((), (), s32[]{:S(2)}) async-start(), calls=%async_computation.1 | async-start | bytes 2621440 | tf_op jit(solution)/shard_map/all_gather | solution.py:94
  9.3 7.0 %copy-start.2 = (s32[1536]{0:T(1024)S(1)}, s32[1536]{0:T(1024)}, u32[]{:S(2)}) copy-start(s32[1536]{0:T(1024)} %param.17) | copy-start | bytes 18436
  9.3 7.0 %copy-start = (bf16[1024,1536]{1,0:T(8,128)(2,1)S(1)}, bf16[1024,1536]{1,0:T(8,128)(2,1)}, u32[]{:S(2)}) copy-start(bf16[1024,1536]{1,0:T(8,128)(2,1)} %param.16) | copy-start | bytes 9437188
  16.3 267.5 %all-gather.5.cloned.1.call-start = ((), (), s32[]{:S(2)}) async-start(), calls=%async_computation | async-start | bytes 15728640 | tf_op jit(solution)/shard_map/all_gather | solution.py:48
  16.4 2.8 copy-start.5
  34.7 32.6 %copy-start.4 = (bf16[256,1024]{1,0:T(8,128)(2,1)S(1)}, bf16[256,1024]{1,0:T(8,128)(2,1)}, u32[]{:S(2)}) copy-start(bf16[256,1024]{1,0:T(8,128)(2,1)} %param.9) | copy-start | bytes 1572868
  68.3 1.0 copy-start.1
  68.3 1.0 copy-start.3
  69.7 8.7 %collective-permute-start = (bf16[256,1024]{1,0:T(8,128)(2,1)S(1)}, bf16[256,1024]{1,0:T(8,128)(2,1)S(1)}, u32[]{:S(2)}, u32[]{:S(2)}) collective-permute-start(bf16[256,1024]{1,0:T(8,128)(2,1)S(1)} %multiply_convert_fusion.2), channel_id=1, source_target_pairs={{0,1},{1,2},{2,3},{3,0},{4,5},{5,6},{6,7},{7,4},{8,9},{9,10},{10,1... | collective-permute-start | bytes 1572872 | tf_op jit(solution)/shard_map/ppermute | solution.py:16
  78.3 12.4 %collective-permute-start.1 = (bf16[256,1024]{1,0:T(8,128)(2,1)S(1)}, bf16[256,1024]{1,0:T(8,128)(2,1)S(1)}, u32[]{:S(2)}, u32[]{:S(2)}) collective-permute-start(bf16[256,1024]{1,0:T(8,128)(2,1)S(1)} %collective-permute-done), channel_id=1, source_target_pairs={{0,1},{1,2},{2,3},{3,0},{4,5},{5,6},{6,7},{7,4},{8,9},{9,10},{10,1... | collective-permute-start | bytes 1572872 | tf_op jit(solution)/shard_map/ppermute | solution.py:16
  78.3 15.1 %collective-permute-start.2 = (bf16[256,1024]{1,0:T(8,128)(2,1)S(1)}, bf16[256,1024]{1,0:T(8,128)(2,1)S(1)}, u32[]{:S(2)}, u32[]{:S(2)}) collective-permute-start(bf16[256,1024]{1,0:T(8,128)(2,1)S(1)} %multiply_convert_fusion.2), channel_id=1, source_target_pairs={{0,3},{1,0},{2,1},{3,2},{4,7},{5,4},{6,5},{7,6},{8,11},{9,8},{10,9... | collective-permute-start | bytes 1572872 | tf_op jit(solution)/shard_map/ppermute | solution.py:18
Sparse Core Ops, SparseCore 0:
  16.4 48.7 all-gather.6
  66.7 216.9 all-gather.4
